TPU v7x, 256 devices: a whole 4x4x8 slice. The times are simulated.
256 devices in a mesh: hyp: 32 (over y, x, core), head: 8 (over z).
Axes of the slice: x: 4, y: 4, z: 8, core: 2. Of those that a mesh axis runs over, the one named last changes fastest.
Arguments:
- step_embeds: bfloat16 [3, 512, 4096], P(None, 'hyp'), may hold values from -6 to 6
- lang_table: bfloat16 [8, 4096], replicated, may hold values from -3 to 3
- lang_ids: int32 [32, 4], replicated, may hold values from 0 to 7
- self_gain: float32 [4096], replicated, may hold values from 0.1 to 1.9
- self_wq: bfloat16 [4096, 2048], P(None, 'head'), may hold values from -0.09375 to 0.09375
- self_wk: bfloat16 [4096, 2048], P(None, 'head'), may hold values from -0.09375 to 0.09375
- self_wv: bfloat16 [4096, 2048], P(None, 'head'), may hold values from -0.09375 to 0.09375
- self_wo: bfloat16 [2048, 4096], P('head'), may hold values from -0.125 to 0.125
- cross_gain: float32 [4096], replicated, may hold values from 0.1 to 1.9
- cross_wq: bfloat16 [4096, 2048], P(None, 'head'), may hold values from -0.09375 to 0.09375
- cross_wkv: bfloat16 [4096, 4096], P('hyp', 'head'), may hold values from -0.09375 to 0.09375
- encoder_rows: bfloat16 [24576, 4096], P('hyp', 'head'), may hold values from -200 to 200
- doc_lengths: int32 [32], P('hyp'), may hold values from 192 to 768, as said below
- past_keys: bfloat16 [512, 32, 2048], P('hyp', None, 'head'), may hold values from -200 to 200
- past_values: bfloat16 [512, 32, 2048], P('hyp', None, 'head'), may hold values from -6 to 6
- parents: int32 [3, 512], replicated, may hold values from 0 to 3
Outputs:
- cross_context: bfloat16 [3, 512, 2048], P(None, 'hyp', 'head')
- final_keys: bfloat16 [512, 35, 2048], P('hyp', None, 'head')
- final_values: bfloat16 [512, 35, 2048], P('hyp', None, 'head')
Inputs may be any that keep to these rules, and one draw needn't show every extreme that they name: `doc_lengths`: some document has exactly 768 live rows. `parents`: A parent is a beam of the same document and target.
All inputs are finite; a program needn't handle non-finite values.
Results may differ from a plain program's by a relative error of at most 0.03.
Values may be sent and summed in bfloat16 or wider, within the bound.
No kernel may reach another device: no remote copies, remote signals or barrier semaphores. Data moves between devices by JAX's collectives and lax.ppermute only.
A program may use at most 128 MiB of HBM per device.

v0:
```python
import jax
import jax.numpy as jnp
from jax import lax
from jax.sharding import PartitionSpec as P

HEAD = 256
BEAMS = 4
TARGETS = 4
STEPS = 3
EPSILON = 1e-06


def shifted(block, axis, distance):
    devices = range(lax.axis_size(axis))
    route = [((i - distance) % len(devices), i) for i in devices]
    return lax.ppermute(block, axis, route)


def rms_scaled(values_in, gain):
    mean_square = jnp.mean(values_in * values_in, axis=-1, keepdims=True)
    return values_in * lax.rsqrt(mean_square + EPSILON) * gain


def pick_rows(candidates, selector, row_axis):
    shape_list = [1] * candidates[0].ndim
    shape_list[row_axis] = selector.shape[0]
    chosen = candidates[0]
    for position in range(1, len(candidates)):
        chosen = jnp.where((selector == position).reshape(shape_list), candidates[position], chosen)
    return chosen


def partial_attend(queries, cache_stack, scaling):
    row_count = cache_stack.shape[1]
    cached = cache_stack.shape[2]
    heads_here = cache_stack.shape[3] // HEAD
    key_part = cache_stack[0].reshape(row_count, cached, heads_here, HEAD)
    value_part = cache_stack[1].reshape(row_count, cached, heads_here, HEAD).astype(jnp.float32)
    scores = (
        jnp.einsum(
            "rhd,rphd->rhp",
            queries.reshape(row_count, heads_here, HEAD),
            key_part,
            preferred_element_type=jnp.float32,
        )
        * scaling
    )
    highest = jnp.max(scores, axis=2)
    raw_weights = jnp.exp(scores - highest[:, :, None])
    totals = jnp.sum(raw_weights, axis=2)
    summed = jnp.einsum("rhp,rphd->rhd", raw_weights, value_part)
    return (highest, totals, summed)


def cross_attend(queries, cross_keys, cross_values, doc_length, scaling):
    query_rows = queries.shape[0]
    heads_here = cross_keys.shape[1]
    scores = (
        jnp.einsum(
            "qhd,jhd->hqj",
            queries.reshape(query_rows, heads_here, HEAD),
            cross_keys,
            preferred_element_type=jnp.float32,
        )
        * scaling
    )
    live_mask = lax.broadcasted_iota(jnp.int32, (1, 1, cross_keys.shape[0]), 2) < doc_length
    scores = jnp.where(live_mask, scores, -jnp.inf)
    highest = jnp.max(scores, axis=2, keepdims=True)
    raw_weights = jnp.exp(scores - highest)
    totals = jnp.sum(raw_weights, axis=2, keepdims=True)
    weights = (raw_weights / totals).astype(jnp.bfloat16)
    output = jnp.einsum("hqj,jhd->qhd", weights, cross_values, preferred_element_type=jnp.float32)
    return output.reshape(query_rows, heads_here * HEAD).astype(jnp.bfloat16)


def shards(
    step_embeds,
    lang_table,
    lang_ids,
    self_gain,
    self_wq,
    self_wk,
    self_wv,
    self_wo,
    cross_gain,
    cross_wq,
    cross_wkv,
    encoder_rows,
    doc_lengths,
    past_keys,
    past_values,
    parents,
):
    hyp_count = lax.axis_size("hyp")
    group_size = hyp_count // BEAMS
    my_index = lax.axis_index("hyp")
    my_beam = my_index // group_size
    my_slot = my_index % group_size
    row_count = step_embeds.shape[1]
    head_width = self_wq.shape[1]
    heads_here = head_width // HEAD
    doc_count = lang_ids.shape[0]
    scaling = HEAD ** (-0.5)
    my_langs = lax.dynamic_slice_in_dim(lang_ids, my_slot * BEAMS, BEAMS, 0).reshape(row_count)
    one_hot = (
        my_langs[:, None] == lax.broadcasted_iota(jnp.int32, (1, lang_table.shape[0]), 1)
    ).astype(jnp.bfloat16)
    lang_rows = jnp.dot(one_hot, lang_table, preferred_element_type=jnp.float32)
    full_weights = lax.all_gather(cross_wkv, "hyp", axis=0, tiled=True)
    cross_kv = jnp.dot(
        lax.all_gather(encoder_rows, "head", axis=1, tiled=True),
        full_weights,
        preferred_element_type=jnp.float32,
    ).astype(jnp.bfloat16)
    cross_kv = cross_kv.reshape(encoder_rows.shape[0], heads_here, 2, HEAD)
    cross_keys = cross_kv[:, :, 0, :]
    cross_values = cross_kv[:, :, 1, :]
    doc_length = doc_lengths[0]
    parent_view = parents.reshape(parents.shape[0], BEAMS, -1)
    my_parents = lax.dynamic_slice_in_dim(parent_view, my_slot * row_count, row_count, 2)
    own_parents = lax.dynamic_index_in_dim(my_parents, my_beam, 1, keepdims=False)
    contexts = []
    cache_stack = jnp.stack([past_keys, past_values])
    for step_idx in range(STEPS):
        offsets = (my_beam - own_parents[step_idx]) % BEAMS
        moved_list = [cache_stack]
        for peer_hop in range(1, BEAMS):
            moved_list.append(shifted(cache_stack, "hyp", peer_hop * group_size))
        cache_stack = pick_rows(moved_list, offsets, 1)
        start_hidden_in = step_embeds[step_idx].astype(jnp.float32) + lang_rows
        normed = rms_scaled(start_hidden_in, self_gain).astype(jnp.bfloat16)
        new_query = jnp.dot(normed, self_wq, preferred_element_type=jnp.float32).astype(
            jnp.bfloat16
        )
        new_key = jnp.dot(normed, self_wk, preferred_element_type=jnp.float32).astype(jnp.bfloat16)
        new_value = jnp.dot(normed, self_wv, preferred_element_type=jnp.float32).astype(
            jnp.bfloat16
        )
        fresh_rows = jnp.stack([new_key, new_value])[:, :, None, :]
        hidden_in, new_query, fresh_rows = (start_hidden_in, new_query, fresh_rows)
        cache_stack = jnp.concatenate([cache_stack, fresh_rows], axis=2)
        attn_parts = partial_attend(new_query, cache_stack, scaling)
        rows_here = hidden_in.shape[0]
        self_context = (
            (attn_parts[2] / attn_parts[1][:, :, None])
            .reshape(rows_here, head_width)
            .astype(jnp.bfloat16)
        )
        partial_out = jnp.dot(self_context, self_wo, preferred_element_type=jnp.float32)
        residual = hidden_in + lax.psum(partial_out.astype(jnp.bfloat16), "head").astype(
            jnp.float32
        )
        normed_cross = rms_scaled(residual, cross_gain).astype(jnp.bfloat16)
        cross_query = jnp.dot(normed_cross, cross_wq, preferred_element_type=jnp.float32).astype(
            jnp.bfloat16
        )
        every_query = lax.all_gather(cross_query, "hyp", axis=0, tiled=True)
        arranged = every_query.reshape(BEAMS, doc_count, TARGETS, head_width)
        doc_queries = lax.dynamic_index_in_dim(arranged, my_index, 1, keepdims=False)
        answer = cross_attend(
            doc_queries.reshape(BEAMS * TARGETS, head_width),
            cross_keys,
            cross_values,
            doc_length,
            scaling,
        )
        every_answer = lax.all_gather(answer, "hyp", axis=0, tiled=True)
        by_owner = every_answer.reshape(doc_count, BEAMS, TARGETS, head_width)
        my_block = lax.dynamic_slice_in_dim(by_owner, my_slot * BEAMS, BEAMS, 0)
        contexts.append(
            lax.dynamic_index_in_dim(my_block, my_beam, 1, keepdims=False).reshape(
                row_count, head_width
            )
        )
    return (jnp.stack(contexts), cache_stack[0], cache_stack[1])


def solution(mesh):
    return jax.shard_map(
        shards,
        mesh=mesh,
        in_specs=(
            P(None, "hyp", None),
            P(),
            P(),
            P(),
            P(None, "head"),
            P(None, "head"),
            P(None, "head"),
            P("head", None),
            P(),
            P(None, "head"),
            P("hyp", "head"),
            P("hyp", "head"),
            P("hyp"),
            P("hyp", None, "head"),
            P("hyp", None, "head"),
            P(),
        ),
        out_specs=(P(None, "hyp", "head"), P("hyp", None, "head"), P("hyp", None, "head")),
        check_vma=False,
    )
```

profile of v0, /device:TPU:1, one launch (start us, length us, event | category | flops | bytes accessed | tf_op | source)
XLA Modules:
  0.0 360.1 jit_solution(13073119696567710992)
XLA Ops:
  8.1 1.5 copy_bitcast_fusion
  10.4 3.6 collective-permute-start
  15.9 2.7 fusion.11
  20.4 1.0 fusion.5
  21.4 1.0 fusion.4
  22.4 2.8 fusion.9
  25.2 1.0 fusion.3
  27.1 8.9 %collective-permute-done = bf16[2,16,32,256]{3,1,2,0:T(8,128)(2,1)} collective-permute-done((bf16[2,16,32,256]{3,1,2,0:T(8,128)(2,1)}, bf16[2,16,32,256]{3,1,2,0:T(8,128)(2,1)}, u32[]{:S(2)}, u32[]{:S(2)}) %collective-permute-start) | collective-permute-done | bytes 524320 | tf_op jit(solution)/shard_map/ppermute | solution.py:16
  36.0 4.9 %collective-permute-done.2 = bf16[2,16,32,256]{3,1,2,0:T(8,128)(2,1)} collective-permute-done((bf16[2,16,32,256]{3,1,2,0:T(8,128)(2,1)}, bf16[2,16,32,256]{3,1,2,0:T(8,128)(2,1)}, u32[]{:S(2)}, u32[]{:S(2)}) %collective-permute-start.2) | collective-permute-done | bytes 524320 | tf_op jit(solution)/shard_map/ppermute | solution.py:16
  40.9 1.5 select_select_fusion.2
  43.0 1.0 collective-permute-start.5
  44.8 1.1 convolution_convert_fusion.2
  45.9 10.0 %collective-permute-done.3 = bf16[2,16,33,256]{3,1,2,0:T(8,128)(2,1)S(1)} collective-permute-done((bf16[2,16,33,256]{3,1,2,0:T(8,128)(2,1)S(1)}, bf16[2,16,33,256]{3,1,2,0:T(8,128)(2,1)S(1)}, u32[]{:S(2)}, u32[]{:S(2)}) %collective-permute-start.3) | collective-permute-done | bytes 540704 | tf_op jit(solution)/shard_map/ppermute | solution.py:16
  55.9 1.1 collective-permute-done.4
  57.0 12.9 %collective-permute-done.5 = bf16[2,16,33,256]{3,1,2,0:T(8,128)(2,1)S(1)} collective-permute-done((bf16[2,16,33,256]{3,1,2,0:T(8,128)(2,1)S(1)}, bf16[2,16,33,256]{3,1,2,0:T(8,128)(2,1)S(1)}, u32[]{:S(2)}, u32[]{:S(2)}) %collective-permute-start.5) | collective-permute-done | bytes 540704 | tf_op jit(solution)/shard_map/ppermute | solution.py:16
  70.7 1.0 collective-permute-start.8
  72.5 1.1 convolution_convert_fusion.1
  73.6 10.3 %collective-permute-done.6 = bf16[2,16,34,256]{3,1,2,0:T(8,128)(2,1)S(1)} collective-permute-done((bf16[2,16,34,256]{3,1,2,0:T(8,128)(2,1)S(1)}, bf16[2,16,34,256]{3,1,2,0:T(8,128)(2,1)S(1)}, u32[]{:S(2)}, u32[]{:S(2)}) %collective-permute-start.6) | collective-permute-done | bytes 557088 | tf_op jit(solution)/shard_map/ppermute | solution.py:16
  84.6 13.7 %collective-permute-done.8 = bf16[2,16,34,256]{3,1,2,0:T(8,128)(2,1)S(1)} collective-permute-done((bf16[2,16,34,256]{3,1,2,0:T(8,128)(2,1)S(1)}, bf16[2,16,34,256]{3,1,2,0:T(8,128)(2,1)S(1)}, u32[]{:S(2)}, u32[]{:S(2)}) %collective-permute-start.8) | collective-permute-done | bytes 557088 | tf_op jit(solution)/shard_map/ppermute | solution.py:16
  99.5 1.1 convolution_convert_fusion
  103.0 72.8 %all-reduce.3.cloned.1.call-done = (bf16[16,4096]{1,0:T(8,128)(2,1)}, bf16[16,4096]{1,0:T(8,128)(2,1)}, bf16[16,4096]{1,0:T(8,128)(2,1)}) async-done(((bf16[16,4096]{1,0:T(8,128)(2,1)}, bf16[16,4096]{1,0:T(8,128)(2,1)}, bf16[16,4096]{1,0:T(8,128)(2,1)}), (bf16[16,4096]{1,0:T(8,128)(2,1)}, bf16[16,4096]{1,0:T(8,128)(2,1)}, bf16[16,4096]{1,0:T(8,128)(2,1)})) %all-reduce.3.cloned.1.call-update) | async-done | bytes 393232 | tf_op jit(solution)/shard_map/psum | solution.py:151
  175.8 1.8 multiply_reduce_fusion.4
  177.6 2.1 convolution_convert_fusion.4
  179.7 37.9 %all_gather.30 = bf16[512,256]{1,0:T(8,128)(2,1)S(1)} all-gather(bf16[16,256]{1,0:T(8,128)(2,1)S(1)} %convolution_convert_fusion.4), channel_id=1, replica_groups=mesh['hyp'=32,'head'=8] {'hyp'}, dimensions={0}, use_global_device_ids=true | all-gather | bytes 270336 | tf_op jit(solution)/shard_map/all_gather | solution.py:158
  218.9 2.0 convolution_convert_fusion.8
  220.9 24.2 %all_gather.28 = bf16[512,256]{1,0:T(8,128)(2,1)S(1)} all-gather(bf16[16,256]{1,0:T(8,128)(2,1)S(1)} %convolution_convert_fusion.8), channel_id=1, replica_groups=mesh['hyp'=32,'head'=8] {'hyp'}, dimensions={0}, use_global_device_ids=true | all-gather | bytes 270336 | tf_op jit(solution)/shard_map/all_gather | solution.py:158
  245.8 2.0 convolution_convert_fusion.12
  247.8 22.6 %all_gather.26 = bf16[512,256]{1,0:T(8,128)(2,1)S(1)} all-gather(bf16[16,256]{1,0:T(8,128)(2,1)S(1)} %convolution_convert_fusion.12), channel_id=1, replica_groups=mesh['hyp'=32,'head'=8] {'hyp'}, dimensions={0}, use_global_device_ids=true | all-gather | bytes 270336 | tf_op jit(solution)/shard_map/all_gather | solution.py:158
  270.7 7.5 %convolution_convert_fusion.3 = bf16[768,512]{0,1:T(8,128)(2,1)S(1)} fusion(bf16[768,4096]{1,0:T(8,128)(2,1)} %all-gather.6.cloned.1.call-done, bf16[4096,512]{1,0:T(8,128)(2,1)} %all-gather.8.cloned.1.call-done), kind=kOutput, calls=%fused_computation.3 | convolution fusion | flops 3221618688 | bytes 11272192 | tf_op jit(solution)/shard_map/dot_general | solution.py:111
  278.9 24.5 %all-gather.2 = bf16[512,1,256]{2,0,1:T(8,128)(2,1)S(1)} all-gather(bf16[16,1,256]{2,0,1:T(8,128)(2,1)S(1)} %fusion.14), channel_id=4, replica_groups=mesh['hyp'=32,'head'=8] {'hyp'}, dimensions={0}, use_global_device_ids=true | all-gather | bytes 270336 | tf_op jit(solution)/shard_map/all_gather | solution.py:168
  304.2 22.7 %all-gather.1 = bf16[512,1,256]{2,0,1:T(8,128)(2,1)S(1)} all-gather(bf16[16,1,256]{2,0,1:T(8,128)(2,1)S(1)} %fusion.13), channel_id=3, replica_groups=mesh['hyp'=32,'head'=8] {'hyp'}, dimensions={0}, use_global_device_ids=true | all-gather | bytes 270336 | tf_op jit(solution)/shard_map/all_gather | solution.py:168
  327.7 24.3 %all-gather = bf16[512,1,256]{2,0,1:T(8,128)(2,1)S(1)} all-gather(bf16[16,1,256]{2,0,1:T(8,128)(2,1)S(1)} %fusion.12), channel_id=2, replica_groups=mesh['hyp'=32,'head'=8] {'hyp'}, dimensions={0}, use_global_device_ids=true | all-gather | bytes 270336 | tf_op jit(solution)/shard_map/all_gather | solution.py:168
  (137 shorter events, 16.9 us)
Async XLA Ops:
  8.0 36.8 %copy-start = (bf16[256,4096]{1,0:T(8,128)(2,1)S(1)}, bf16[256,4096]{1,0:T(8,128)(2,1)}, u32[]{:S(2)}) copy-start(bf16[256,4096]{1,0:T(8,128)(2,1)} %param.23) | copy-start | bytes 6291460
  8.0 7.0 %copy-start.22 = (s32[32,4]{0,1:T(4,128)S(1)}, s32[32,4]{0,1:T(4,128)}, u32[]{:S(2)}) copy-start(s32[32,4]{0,1:T(4,128)} %param.18) | copy-start | bytes 1540
  8.0 7.2 %copy-start.4 = (bf16[3,16,4096]{2,1,0:T(8,128)(2,1)S(1)}, bf16[3,16,4096]{2,1,0:T(8,128)(2,1)}, u32[]{:S(2)}) copy-start(bf16[3,16,4096]{2,1,0:T(8,128)(2,1)} %param.16) | copy-start | bytes 1179652
  8.0 7.2 %copy-start.24 = (bf16[8,4096]{1,0:T(8,128)(2,1)S(1)}, bf16[8,4096]{1,0:T(8,128)(2,1)}, u32[]{:S(2)}) copy-start(bf16[8,4096]{1,0:T(8,128)(2,1)} %param.17) | copy-start | bytes 196612
  8.0 7.7 %copy-start.17 = (f32[4096]{0:T(1024)S(1)}, f32[4096]{0:T(1024)}, u32[]{:S(2)}) copy-start(f32[4096]{0:T(1024)} %param.19) | copy-start | bytes 49156
  8.1 167.7 %all-reduce.3.cloned.1.call-start = ((), (), s32[]{:S(2)}) async-start(), calls=%async_computation.2 | async-start | bytes 786432 | tf_op jit(solution)/shard_map/psum | solution.py:151
  10.4 25.6 %collective-permute-start = (bf16[2,16,32,256]{3,1,2,0:T(8,128)(2,1)}, bf16[2,16,32,256]{3,1,2,0:T(8,128)(2,1)}, u32[]{:S(2)}, u32[]{:S(2)}) collective-permute-start(bf16[2,16,32,256]{3,1,2,0:T(8,128)(2,1)} %pad_maximum_fusion.2), channel_id=1, source_target_pairs={{64,0},{72,8},{80,16},{88,24},{96,32},{104,40},{112,48},{120,56},{... | collective-permute-start | bytes 1572872 | tf_op jit(solution)/shard_map/ppermute | solution.py:16
  14.0 22.0 %collective-permute-start.1 = (bf16[2,16,32,256]{3,1,2,0:T(8,128)(2,1)}, bf16[2,16,32,256]{3,1,2,0:T(8,128)(2,1)}, u32[]{:S(2)}, u32[]{:S(2)}) collective-permute-start(bf16[2,16,32,256]{3,1,2,0:T(8,128)(2,1)} %pad_maximum_fusion.2), channel_id=1, source_target_pairs={{128,0},{136,8},{144,16},{152,24},{160,32},{168,40},{176,48},{184,... | collective-permute-start | bytes 1572872 | tf_op jit(solution)/shard_map/ppermute | solution.py:16
  14.3 26.6 %collective-permute-start.2 = (bf16[2,16,32,256]{3,1,2,0:T(8,128)(2,1)}, bf16[2,16,32,256]{3,1,2,0:T(8,128)(2,1)}, u32[]{:S(2)}, u32[]{:S(2)}) collective-permute-start(bf16[2,16,32,256]{3,1,2,0:T(8,128)(2,1)} %pad_maximum_fusion.2), channel_id=1, source_target_pairs={{192,0},{200,8},{208,16},{216,24},{224,32},{232,40},{240,48},{248,... | collective-permute-start | bytes 1572872 | tf_op jit(solution)/shard_map/ppermute | solution.py:16
  15.3 3.4 copy-start.2
  15.9 3.7 %copy-start.5 = (bf16[16,4096]{1,0:T(8,128)(2,1)}, bf16[16,4096]{1,0:T(8,128)(2,1)S(1)}, u32[]{:S(2)}) copy-start(bf16[16,4096]{1,0:T(8,128)(2,1)S(1)} %get-tuple-element.24) | copy-start | bytes 393220
  15.9 3.7 %copy-start.1 = (bf16[4096,256]{1,0:T(8,128)(2,1)S(1)}, bf16[4096,256]{1,0:T(8,128)(2,1)}, u32[]{:S(2)}) copy-start(bf16[4096,256]{1,0:T(8,128)(2,1)} %param.22) | copy-start | bytes 6291460
  22.4 2.8 copy-start.3
  26.2 0.9 copy-start.14
  40.9 3.2 copy-start.20
  42.5 13.4 %collective-permute-start.3 = (bf16[2,16,33,256]{3,1,2,0:T(8,128)(2,1)S(1)}, bf16[2,16,33,256]{3,1,2,0:T(8,128)(2,1)S(1)}, u32[]{:S(2)}, u32[]{:S(2)}) collective-permute-start(bf16[2,16,33,256]{3,1,2,0:T(8,128)(2,1)S(1)} %pad_maximum_fusion.1), channel_id=1, source_target_pairs={{64,0},{72,8},{80,16},{88,24},{96,32},{104,40},{112,48},{120,56},{... | collective-permute-start | bytes 1622024 | tf_op jit(solution)/shard_map/ppermute | solution.py:16
  42.6 14.5 %collective-permute-start.4 = (bf16[2,16,33,256]{3,1,2,0:T(8,128)(2,1)S(1)}, bf16[2,16,33,256]{3,1,2,0:T(8,128)(2,1)S(1)}, u32[]{:S(2)}, u32[]{:S(2)}) collective-permute-start(bf16[2,16,33,256]{3,1,2,0:T(8,128)(2,1)S(1)} %pad_maximum_fusion.1), channel_id=1, source_target_pairs={{128,0},{136,8},{144,16},{152,24},{160,32},{168,40},{176,48},{184,... | collective-permute-start | bytes 1622024 | tf_op jit(solution)/shard_map/ppermute | solution.py:16
  43.0 26.9 %collective-permute-start.5 = (bf16[2,16,33,256]{3,1,2,0:T(8,128)(2,1)S(1)}, bf16[2,16,33,256]{3,1,2,0:T(8,128)(2,1)S(1)}, u32[]{:S(2)}, u32[]{:S(2)}) collective-permute-start(bf16[2,16,33,256]{3,1,2,0:T(8,128)(2,1)S(1)} %pad_maximum_fusion.1), channel_id=1, source_target_pairs={{192,0},{200,8},{208,16},{216,24},{224,32},{232,40},{240,48},{248,... | collective-permute-start | bytes 1622024 | tf_op jit(solution)/shard_map/ppermute | solution.py:16
  70.2 13.8 %collective-permute-start.6 = (bf16[2,16,34,256]{3,1,2,0:T(8,128)(2,1)S(1)}, bf16[2,16,34,256]{3,1,2,0:T(8,128)(2,1)S(1)}, u32[]{:S(2)}, u32[]{:S(2)}) collective-permute-start(bf16[2,16,34,256]{3,1,2,0:T(8,128)(2,1)S(1)} %pad_maximum_fusion), channel_id=1, source_target_pairs={{64,0},{72,8},{80,16},{88,24},{96,32},{104,40},{112,48},{120,56},{... | collective-permute-start | bytes 1671176 | tf_op jit(solution)/shard_map/ppermute | solution.py:16
  70.2 14.4 %collective-permute-start.7 = (bf16[2,16,34,256]{3,1,2,0:T(8,128)(2,1)S(1)}, bf16[2,16,34,256]{3,1,2,0:T(8,128)(2,1)S(1)}, u32[]{:S(2)}, u32[]{:S(2)}) collective-permute-start(bf16[2,16,34,256]{3,1,2,0:T(8,128)(2,1)S(1)} %pad_maximum_fusion), channel_id=1, source_target_pairs={{128,0},{136,8},{144,16},{152,24},{160,32},{168,40},{176,48},{184,... | collective-permute-start | bytes 1671176 | tf_op jit(solution)/shard_map/ppermute | solution.py:16
  70.7 27.6 %collective-permute-start.8 = (bf16[2,16,34,256]{3,1,2,0:T(8,128)(2,1)S(1)}, bf16[2,16,34,256]{3,1,2,0:T(8,128)(2,1)S(1)}, u32[]{:S(2)}, u32[]{:S(2)}) collective-permute-start(bf16[2,16,34,256]{3,1,2,0:T(8,128)(2,1)S(1)} %pad_maximum_fusion), channel_id=1, source_target_pairs={{192,0},{200,8},{208,16},{216,24},{224,32},{232,40},{240,48},{248,... | collective-permute-start | bytes 1671176 | tf_op jit(solution)/shard_map/ppermute | solution.py:16
  73.6 25.0 %copy-start.19 = (bf16[16,256,1]{1,0,2:T(8,128)(2,1)S(1)}, bf16[16,256,1]{1,0,2:T(8,128)(2,1)}, u32[]{:S(2)}) copy-start(bf16[16,256,1]{1,0,2:T(8,128)(2,1)} %fusion.9) | copy-start | bytes 24580
  98.6 0.9 copy-start.9
  99.5 78.1 %copy-start.10 = (f32[4096]{0:T(1024)S(1)}, f32[4096]{0:T(1024)}, u32[]{:S(2)}) copy-start(f32[4096]{0:T(1024)} %param.24) | copy-start | bytes 49156
  100.6 170.0 %all-gather.8.cloned.1.call-start = ((), (), s32[]{:S(2)}) async-start(), calls=%async_computation.1 | async-start | bytes 4325376 | tf_op jit(solution)/shard_map/all_gather | solution.py:110
  101.2 169.5 %all-gather.6.cloned.1.call-start = ((), (), s32[]{:S(2)}) async-start(), calls=%async_computation | async-start | bytes 7077888 | tf_op jit(solution)/shard_map/all_gather | solution.py:112
  175.8 43.1 %copy-start.8 = (bf16[16,4096]{1,0:T(8,128)(2,1)S(1)}, bf16[16,4096]{1,0:T(8,128)(2,1)}, u32[]{:S(2)}) copy-start(bf16[16,4096]{1,0:T(8,128)(2,1)} %get-tuple-element.11) | copy-start | bytes 393220
  179.7 66.1 %copy-start.7 = (bf16[16,4096]{1,0:T(8,128)(2,1)S(1)}, bf16[16,4096]{1,0:T(8,128)(2,1)}, u32[]{:S(2)}) copy-start(bf16[16,4096]{1,0:T(8,128)(2,1)} %get-tuple-element.10) | copy-start | bytes 393220
  217.7 28.1 %copy-start.23 = (f32[16]{0:T(128)S(1)}, f32[16]{0:T(128)}, u32[]{:S(2)}) copy-start(f32[16]{0:T(128)} %get-tuple-element.3) | copy-start | bytes 196
  270.6 7.6 %copy-start.12 = (bf16[16,256]{1,0:T(8,128)(2,1)S(1)}, bf16[16,256]{1,0:T(8,128)(2,1)}, u32[]{:S(2)}) copy-start(bf16[16,256]{1,0:T(8,128)(2,1)} %reshape.403) | copy-start | bytes 24580
  270.6 7.6 %copy-start.18 = (pred[768]{0:T(1024)(128)(4,1)S(1)}, pred[768]{0:T(1024)(128)(4,1)}, u32[]{:S(2)}) copy-start(pred[768]{0:T(1024)(128)(4,1)} %iota_compare_fusion.2) | copy-start | bytes 2308
  270.6 32.9 %copy-start.11 = (bf16[16,256]{1,0:T(8,128)(2,1)S(1)}, bf16[16,256]{1,0:T(8,128)(2,1)}, u32[]{:S(2)}) copy-start(bf16[16,256]{1,0:T(8,128)(2,1)} %reshape.398) | copy-start | bytes 24580
  (5 other events, 3.9 us)
Sparse Core Ops, SparseCore 0:
  100.7 74.9 all-reduce.2
Sparse Core Ops, SparseCore 1:
  103.7 52.1 all-gather.7
  157.5 73.3 all-gather.5
where the time goes:
time: 360 us
  blocking collectives  156 us (43%)
  waiting for transfers between devices  136 us (38%)
  matrix products  30.7 us (9%)
  between operations  16.7 us (5%)
  other arithmetic  8.37 us (2%)
  starting transfers between devices  7.79 us (2%)
  local copies, waits for them, and re-layouts  4.05 us (1%)
    all_gather x3, blocking collectives, shards(): every_query = lax.all_gather(cross_query, 'hyp', axis=0, tiled=True)  84.7 us
    psum x1, waiting for transfers between devices, shards(): lax.psum(partial_out.astype(jnp.bfloat16), 'head').astype(jnp.float32)  72.8 us
    all_gather x3, blocking collectives, shards(): every_answer = lax.all_gather(answer, 'hyp', axis=0, tiled=True)  71.4 us
    ppermute x9, waiting for transfers between devices, shifted(): return lax.ppermute(block, axis, route)  62.5 us
    ppermute x9, starting transfers between devices, shifted(): return lax.ppermute(block, axis, route)  7.67 us
    dot_general x1, matrix products, shards(): jnp.dot(lax.all_gather(encoder_rows, 'head', axis=1, tiled=True), full_we...  7.47 us
  transfers between devices with their start and end apart: 12, of which 9 were waited for; matrix products, arithmetic and copies ran while one was open for 7% of the time, Pallas kernels for 0%

commit v1 on v0

--- a/solution.py
+++ b/solution.py
@@ -1,3 +1,4 @@
+import functools
 import jax
 import jax.numpy as jnp
 from jax import lax
@@ -8,6 +9,13 @@
 TARGETS = 4
 STEPS = 3
 EPSILON = 1e-06
+
+
+def rails_advance(vector, across):
+    return jnp.sum(lax.all_gather(vector, across), 0)
+
+
+follow_paths_on_mesh = functools.partial(rails_advance, across="head")
 
 
 def shifted(block, axis, distance):
@@ -148,7 +156,7 @@
             .astype(jnp.bfloat16)
         )
         partial_out = jnp.dot(self_context, self_wo, preferred_element_type=jnp.float32)
-        residual = hidden_in + lax.psum(partial_out.astype(jnp.bfloat16), "head").astype(
+        residual = hidden_in + follow_paths_on_mesh(partial_out.astype(jnp.bfloat16)).astype(
             jnp.float32
         )
         normed_cross = rms_scaled(residual, cross_gain).astype(jnp.bfloat16)

time: 360 us -> 385 us (1.069)
  waiting for transfers between devices: 136 us -> 159 us
  other arithmetic: 8.37 us -> 17.5 us
  blocking collectives: 156 us -> 150 us
    psum x1 -> x0, waiting for transfers between devices: 72.8 us -> none  [shards(): lax.psum(partial_out.astype(jnp.bfloat16), 'head').astype(jnp.float32)]
    all_gather x0 -> x3, waiting for transfers between devices: none -> 51.3 us  [rails_advance(): return jnp.sum(lax.all_gather(vector, across), 0)]
    all_gather x1, waiting for transfers between devices: 0.02 us -> 46.2 us  [shards(): lax.all_gather(encoder_rows, 'head', axis=1, tiled=True)]
    all_gather x3, blocking collectives: 84.7 us -> 77.2 us  [shards(): every_query = lax.all_gather(cross_query, 'hyp', axis=0, tiled=True)]
    reduce_sum x0 -> x3, other arithmetic: none -> 4.15 us  [rails_advance(): return jnp.sum(lax.all_gather(vector, across), 0)]
  transfers between devices with their start and end apart: 12 -> 14, of which waited for: 9 -> 11; matrix products, arithmetic and copies ran while one was open for 7% -> 9% of each run, Pallas kernels for 0% -> 0%
where the time goes in v1:
time: 385 us; the launch traced here: 384 us
  waiting for transfers between devices  159 us (41%)
  blocking collectives  150 us (39%)
  matrix products  31.8 us (8%)
  other arithmetic  17.5 us (5%)
  between operations  14.9 us (4%)
  starting transfers between devices  7.91 us (2%)
    all_gather x3, blocking collectives, shards(): every_query = lax.all_gather(cross_query, 'hyp', axis=0, tiled=True)  77.2 us
    all_gather x3, blocking collectives, shards(): every_answer = lax.all_gather(answer, 'hyp', axis=0, tiled=True)  72.8 us
    ppermute x9, waiting for transfers between devices, shifted(): return lax.ppermute(block, axis, route)  60.1 us
    all_gather x3, waiting for transfers between devices, rails_advance(): return jnp.sum(lax.all_gather(vector, across), 0)  51.3 us
    all_gather x1, waiting for transfers between devices, shards(): lax.all_gather(encoder_rows, 'head', axis=1, tiled=True)  46.2 us
  transfers between devices with their start and end apart: 14, of which 11 were waited for; matrix products, arithmetic and copies ran while one was open for 9% of the time, Pallas kernels for 0%

profile of v1, /device:TPU:1, one launch (start us, length us, event | category | flops | bytes accessed | tf_op | source)
XLA Modules:
  0.0 384.1 jit_solution(11741894073573335906)
XLA Ops:
  7.3 1.5 copy_bitcast_fusion
  10.3 3.6 collective-permute-start
  15.8 2.7 fusion.11
  21.1 2.6 fusion.3
  25.5 10.4 %collective-permute-done = bf16[2,16,32,256]{3,1,2,0:T(8,128)(2,1)} collective-permute-done((bf16[2,16,32,256]{3,1,2,0:T(8,128)(2,1)}, bf16[2,16,32,256]{3,1,2,0:T(8,128)(2,1)}, u32[]{:S(2)}, u32[]{:S(2)}) %collective-permute-start) | collective-permute-done | bytes 524320 | tf_op jit(solution)/shard_map/ppermute | solution.py:24
  35.9 4.9 %collective-permute-done.2 = bf16[2,16,32,256]{3,1,2,0:T(8,128)(2,1)} collective-permute-done((bf16[2,16,32,256]{3,1,2,0:T(8,128)(2,1)}, bf16[2,16,32,256]{3,1,2,0:T(8,128)(2,1)}, u32[]{:S(2)}, u32[]{:S(2)}) %collective-permute-start.2) | collective-permute-done | bytes 524320 | tf_op jit(solution)/shard_map/ppermute | solution.py:24
  40.7 1.5 select_select_fusion.2
  43.5 1.1 collective-permute-start.5
  46.6 2.0 fusion.6
  48.6 8.2 %collective-permute-done.3 = bf16[2,16,33,256]{3,1,2,0:T(8,128)(2,1)} collective-permute-done((bf16[2,16,33,256]{3,1,2,0:T(8,128)(2,1)}, bf16[2,16,33,256]{3,1,2,0:T(8,128)(2,1)}, u32[]{:S(2)}, u32[]{:S(2)}) %collective-permute-start.3) | collective-permute-done | bytes 540704 | tf_op jit(solution)/shard_map/ppermute | solution.py:24
  57.7 13.0 %collective-permute-done.5 = bf16[2,16,33,256]{3,1,2,0:T(8,128)(2,1)} collective-permute-done((bf16[2,16,33,256]{3,1,2,0:T(8,128)(2,1)}, bf16[2,16,33,256]{3,1,2,0:T(8,128)(2,1)}, u32[]{:S(2)}, u32[]{:S(2)}) %collective-permute-start.5) | collective-permute-done | bytes 540704 | tf_op jit(solution)/shard_map/ppermute | solution.py:24
  70.7 1.5 select_select_fusion.1
  76.8 2.0 fusion.9
  78.8 8.3 %collective-permute-done.6 = bf16[2,16,34,256]{3,1,2,0:T(8,128)(2,1)} collective-permute-done((bf16[2,16,34,256]{3,1,2,0:T(8,128)(2,1)}, bf16[2,16,34,256]{3,1,2,0:T(8,128)(2,1)}, u32[]{:S(2)}, u32[]{:S(2)}) %collective-permute-start.6) | collective-permute-done | bytes 557088 | tf_op jit(solution)/shard_map/ppermute | solution.py:24
  87.6 13.9 %collective-permute-done.8 = bf16[2,16,34,256]{3,1,2,0:T(8,128)(2,1)} collective-permute-done((bf16[2,16,34,256]{3,1,2,0:T(8,128)(2,1)}, bf16[2,16,34,256]{3,1,2,0:T(8,128)(2,1)}, u32[]{:S(2)}, u32[]{:S(2)}) %collective-permute-start.8) | collective-permute-done | bytes 557088 | tf_op jit(solution)/shard_map/ppermute | solution.py:24
  101.5 1.6 select_select_fusion
  107.6 1.4 reduce_sum.146
  109.0 14.0 %all-gather.18.cloned.1.call-done = bf16[128,4096]{1,0:T(8,128)(2,1)} async-done(((bf16[16,4096]{1,0:T(8,128)(2,1)}), bf16[128,4096]{1,0:T(8,128)(2,1)}) %all-gather.18.cloned.1.call-update) | async-done | bytes 1048592 | tf_op jit(solution)/shard_map/all_gather | solution.py:15
  123.0 1.4 reduce_sum.151
  124.4 37.3 %all-gather.20.cloned.1.call-done = bf16[128,4096]{1,0:T(8,128)(2,1)} async-done(((bf16[16,4096]{1,0:T(8,128)(2,1)}), bf16[128,4096]{1,0:T(8,128)(2,1)}) %all-gather.20.cloned.1.call-update) | async-done | bytes 1048592 | tf_op jit(solution)/shard_map/all_gather | solution.py:15
  161.7 1.4 reduce_sum.156
  163.9 2.0 convolution_convert_fusion.4
  165.9 30.4 %all_gather.54 = bf16[512,256]{1,0:T(8,128)(2,1)S(1)} all-gather(bf16[16,256]{1,0:T(8,128)(2,1)S(1)} %convolution_convert_fusion.4), channel_id=1, replica_groups=mesh['hyp'=32,'head'=8] {'hyp'}, dimensions={0}, use_global_device_ids=true | all-gather | bytes 270336 | tf_op jit(solution)/shard_map/all_gather | solution.py:166
  197.0 2.0 convolution_convert_fusion.8
  199.0 24.2 %all_gather.50 = bf16[512,256]{1,0:T(8,128)(2,1)S(1)} all-gather(bf16[16,256]{1,0:T(8,128)(2,1)S(1)} %convolution_convert_fusion.8), channel_id=1, replica_groups=mesh['hyp'=32,'head'=8] {'hyp'}, dimensions={0}, use_global_device_ids=true | all-gather | bytes 270336 | tf_op jit(solution)/shard_map/all_gather | solution.py:166
  223.4 2.0 convolution_convert_fusion.12
  225.4 22.6 %all_gather.46 = bf16[512,256]{1,0:T(8,128)(2,1)S(1)} all-gather(bf16[16,256]{1,0:T(8,128)(2,1)S(1)} %convolution_convert_fusion.12), channel_id=1, replica_groups=mesh['hyp'=32,'head'=8] {'hyp'}, dimensions={0}, use_global_device_ids=true | all-gather | bytes 270336 | tf_op jit(solution)/shard_map/all_gather | solution.py:166
  248.1 46.2 %all-gather.12.cloned.1.call-done = bf16[768,4096]{1,0:T(8,128)(2,1)} async-done(((bf16[768,512]{1,0:T(8,128)(2,1)}), bf16[768,4096]{1,0:T(8,128)(2,1)}) %all-gather.12.cloned.1.call-update) | async-done | bytes 6291472 | tf_op jit(solution)/shard_map/all_gather | solution.py:120
  294.3 7.5 %convolution_convert_fusion.3 = bf16[768,512]{0,1:T(8,128)(2,1)S(1)} fusion(bf16[768,4096]{1,0:T(8,128)(2,1)} %all-gather.12.cloned.1.call-done, bf16[4096,512]{1,0:T(8,128)(2,1)} %all-gather.14.cloned.1.call-done), kind=kOutput, calls=%fused_computation.3 | convolution fusion | flops 3221618688 | bytes 11272192 | tf_op jit(solution)/shard_map/dot_general | solution.py:119
  302.5 25.8 %all-gather.5 = bf16[512,1,256]{2,0,1:T(8,128)(2,1)S(1)} all-gather(bf16[16,1,256]{2,0,1:T(8,128)(2,1)S(1)} %fusion.14), channel_id=7, replica_groups=mesh['hyp'=32,'head'=8] {'hyp'}, dimensions={0}, use_global_device_ids=true | all-gather | bytes 270336 | tf_op jit(solution)/shard_map/all_gather | solution.py:176
  329.1 24.2 %all-gather.3 = bf16[512,1,256]{2,0,1:T(8,128)(2,1)S(1)} all-gather(bf16[16,1,256]{2,0,1:T(8,128)(2,1)S(1)} %fusion.13), channel_id=5, replica_groups=mesh['hyp'=32,'head'=8] {'hyp'}, dimensions={0}, use_global_device_ids=true | all-gather | bytes 270336 | tf_op jit(solution)/shard_map/all_gather | solution.py:176
  354.1 22.7 %all-gather.1 = bf16[512,1,256]{2,0,1:T(8,128)(2,1)S(1)} all-gather(bf16[16,1,256]{2,0,1:T(8,128)(2,1)S(1)} %fusion.12), channel_id=3, replica_groups=mesh['hyp'=32,'head'=8] {'hyp'}, dimensions={0}, use_global_device_ids=true | all-gather | bytes 270336 | tf_op jit(solution)/shard_map/all_gather | solution.py:176
  (152 shorter events, 25.3 us)
Async XLA Ops:
  7.2 38.3 %copy-start = (bf16[256,4096]{1,0:T(8,128)(2,1)S(1)}, bf16[256,4096]{1,0:T(8,128)(2,1)}, u32[]{:S(2)}) copy-start(bf16[256,4096]{1,0:T(8,128)(2,1)} %param.23) | copy-start | bytes 6291460
  7.2 7.7 %copy-start.23 = (s32[32,4]{0,1:T(4,128)S(1)}, s32[32,4]{0,1:T(4,128)}, u32[]{:S(2)}) copy-start(s32[32,4]{0,1:T(4,128)} %param.18) | copy-start | bytes 1540
  7.2 7.9 %copy-start.3 = (bf16[3,16,4096]{2,1,0:T(8,128)(2,1)S(1)}, bf16[3,16,4096]{2,1,0:T(8,128)(2,1)}, u32[]{:S(2)}) copy-start(bf16[3,16,4096]{2,1,0:T(8,128)(2,1)} %param.16) | copy-start | bytes 1179652
  7.2 7.9 %copy-start.27 = (bf16[8,4096]{1,0:T(8,128)(2,1)S(1)}, bf16[8,4096]{1,0:T(8,128)(2,1)}, u32[]{:S(2)}) copy-start(bf16[8,4096]{1,0:T(8,128)(2,1)} %param.17) | copy-start | bytes 196612
  7.2 8.4 %copy-start.19 = (f32[4096]{0:T(1024)S(1)}, f32[4096]{0:T(1024)}, u32[]{:S(2)}) copy-start(f32[4096]{0:T(1024)} %param.19) | copy-start | bytes 49156
  7.2 100.4 %all-gather.16.cloned.1.call-start = ((), (), s32[]{:S(2)}) async-start(), calls=%async_computation.2 | async-start | bytes 1179648 | tf_op jit(solution)/shard_map/all_gather | solution.py:15
  10.3 25.6 %collective-permute-start = (bf16[2,16,32,256]{3,1,2,0:T(8,128)(2,1)}, bf16[2,16,32,256]{3,1,2,0:T(8,128)(2,1)}, u32[]{:S(2)}, u32[]{:S(2)}) collective-permute-start(bf16[2,16,32,256]{3,1,2,0:T(8,128)(2,1)} %pad_maximum_fusion.2), channel_id=1, source_target_pairs={{64,0},{72,8},{80,16},{88,24},{96,32},{104,40},{112,48},{120,56},{... | collective-permute-start | bytes 1572872 | tf_op jit(solution)/shard_map/ppermute | solution.py:24
  13.8 22.0 %collective-permute-start.1 = (bf16[2,16,32,256]{3,1,2,0:T(8,128)(2,1)}, bf16[2,16,32,256]{3,1,2,0:T(8,128)(2,1)}, u32[]{:S(2)}, u32[]{:S(2)}) collective-permute-start(bf16[2,16,32,256]{3,1,2,0:T(8,128)(2,1)} %pad_maximum_fusion.2), channel_id=1, source_target_pairs={{128,0},{136,8},{144,16},{152,24},{160,32},{168,40},{176,48},{184,... | collective-permute-start | bytes 1572872 | tf_op jit(solution)/shard_map/ppermute | solution.py:24
  14.2 26.6 %collective-permute-start.2 = (bf16[2,16,32,256]{3,1,2,0:T(8,128)(2,1)}, bf16[2,16,32,256]{3,1,2,0:T(8,128)(2,1)}, u32[]{:S(2)}, u32[]{:S(2)}) collective-permute-start(bf16[2,16,32,256]{3,1,2,0:T(8,128)(2,1)} %pad_maximum_fusion.2), channel_id=1, source_target_pairs={{192,0},{200,8},{208,16},{216,24},{224,32},{232,40},{240,48},{248,... | collective-permute-start | bytes 1572872 | tf_op jit(solution)/shard_map/ppermute | solution.py:24
  15.8 4.1 %copy-start.9 = (bf16[16,4096]{1,0:T(8,128)(2,1)}, bf16[16,4096]{1,0:T(8,128)(2,1)S(1)}, u32[]{:S(2)}) copy-start(bf16[16,4096]{1,0:T(8,128)(2,1)S(1)} %get-tuple-element.22) | copy-start | bytes 393220
  15.8 3.7 copy-start.1
  20.7 20.1 %copy-start.6 = (bf16[1,16,32,256]{3,1,2,0:T(8,128)(2,1)S(1)}, bf16[1,16,32,256]{3,1,2,0:T(8,128)(2,1)}, u32[]{:S(2)}) copy-start(bf16[1,16,32,256]{3,1,2,0:T(8,128)(2,1)} %copy-done.5) | copy-start | bytes 786436
  20.7 20.1 %copy-start.8 = (bf16[1,16,32,256]{3,1,2,0:T(8,128)(2,1)S(1)}, bf16[1,16,32,256]{3,1,2,0:T(8,128)(2,1)}, u32[]{:S(2)}) copy-start(bf16[1,16,32,256]{3,1,2,0:T(8,128)(2,1)} %copy-done.7) | copy-start | bytes 786436
  24.3 20.4 %copy-start.15 = (bf16[2,16,1,256]{3,1,2,0:T(8,128)(2,1)}, bf16[2,16,1,256]{3,1,2,0:T(8,128)(2,1)S(1)}, u32[]{:S(2)}) copy-start(bf16[2,16,1,256]{3,1,2,0:T(8,128)(2,1)S(1)} %maximum_bitcast_fusion) | copy-start | bytes 49156
  40.7 3.9 %copy-start.21 = (bf16[16,256,1]{1,0,2:T(8,128)(2,1)S(1)}, bf16[16,256,1]{1,0,2:T(8,128)(2,1)}, u32[]{:S(2)}) copy-start(bf16[16,256,1]{1,0,2:T(8,128)(2,1)} %fusion.3) | copy-start | bytes 24580
  43.1 13.7 %collective-permute-start.3 = (bf16[2,16,33,256]{3,1,2,0:T(8,128)(2,1)}, bf16[2,16,33,256]{3,1,2,0:T(8,128)(2,1)}, u32[]{:S(2)}, u32[]{:S(2)}) collective-permute-start(bf16[2,16,33,256]{3,1,2,0:T(8,128)(2,1)} %pad_maximum_fusion.1), channel_id=1, source_target_pairs={{64,0},{72,8},{80,16},{88,24},{96,32},{104,40},{112,48},{120,56},{... | collective-permute-start | bytes 1622024 | tf_op jit(solution)/shard_map/ppermute | solution.py:24
  43.1 14.6 %collective-permute-start.4 = (bf16[2,16,33,256]{3,1,2,0:T(8,128)(2,1)}, bf16[2,16,33,256]{3,1,2,0:T(8,128)(2,1)}, u32[]{:S(2)}, u32[]{:S(2)}) collective-permute-start(bf16[2,16,33,256]{3,1,2,0:T(8,128)(2,1)} %pad_maximum_fusion.1), channel_id=1, source_target_pairs={{128,0},{136,8},{144,16},{152,24},{160,32},{168,40},{176,48},{184,... | collective-permute-start | bytes 1622024 | tf_op jit(solution)/shard_map/ppermute | solution.py:24
  43.5 27.3 %collective-permute-start.5 = (bf16[2,16,33,256]{3,1,2,0:T(8,128)(2,1)}, bf16[2,16,33,256]{3,1,2,0:T(8,128)(2,1)}, u32[]{:S(2)}, u32[]{:S(2)}) collective-permute-start(bf16[2,16,33,256]{3,1,2,0:T(8,128)(2,1)} %pad_maximum_fusion.1), channel_id=1, source_target_pairs={{192,0},{200,8},{208,16},{216,24},{224,32},{232,40},{240,48},{248,... | collective-permute-start | bytes 1622024 | tf_op jit(solution)/shard_map/ppermute | solution.py:24
  46.5 76.5 %all-gather.18.cloned.1.call-start = ((), (), s32[]{:S(2)}) async-start(), calls=%async_computation.3 | async-start | bytes 1179648 | tf_op jit(solution)/shard_map/all_gather | solution.py:15
  46.6 25.7 %copy-start.13 = (bf16[2,16,1,256]{3,1,2,0:T(8,128)(2,1)S(1)}, bf16[2,16,1,256]{3,1,2,0:T(8,128)(2,1)}, u32[]{:S(2)}) copy-start(bf16[2,16,1,256]{3,1,2,0:T(8,128)(2,1)} %maximum_bitcast_fusion.1) | copy-start | bytes 49156
  73.2 14.0 %collective-permute-start.6 = (bf16[2,16,34,256]{3,1,2,0:T(8,128)(2,1)}, bf16[2,16,34,256]{3,1,2,0:T(8,128)(2,1)}, u32[]{:S(2)}, u32[]{:S(2)}) collective-permute-start(bf16[2,16,34,256]{3,1,2,0:T(8,128)(2,1)} %pad_maximum_fusion), channel_id=1, source_target_pairs={{64,0},{72,8},{80,16},{88,24},{96,32},{104,40},{112,48},{120,56},{... | collective-permute-start | bytes 1671176 | tf_op jit(solution)/shard_map/ppermute | solution.py:24
  73.2 14.4 %collective-permute-start.7 = (bf16[2,16,34,256]{3,1,2,0:T(8,128)(2,1)}, bf16[2,16,34,256]{3,1,2,0:T(8,128)(2,1)}, u32[]{:S(2)}, u32[]{:S(2)}) collective-permute-start(bf16[2,16,34,256]{3,1,2,0:T(8,128)(2,1)} %pad_maximum_fusion), channel_id=1, source_target_pairs={{128,0},{136,8},{144,16},{152,24},{160,32},{168,40},{176,48},{184,... | collective-permute-start | bytes 1671176 | tf_op jit(solution)/shard_map/ppermute | solution.py:24
  73.5 28.0 %collective-permute-start.8 = (bf16[2,16,34,256]{3,1,2,0:T(8,128)(2,1)}, bf16[2,16,34,256]{3,1,2,0:T(8,128)(2,1)}, u32[]{:S(2)}, u32[]{:S(2)}) collective-permute-start(bf16[2,16,34,256]{3,1,2,0:T(8,128)(2,1)} %pad_maximum_fusion), channel_id=1, source_target_pairs={{192,0},{200,8},{208,16},{216,24},{224,32},{232,40},{240,48},{248,... | collective-permute-start | bytes 1671176 | tf_op jit(solution)/shard_map/ppermute | solution.py:24
  75.4 26.1 %copy-start.14 = (bf16[2,16,1,256]{3,1,2,0:T(8,128)(2,1)S(1)}, bf16[2,16,1,256]{3,1,2,0:T(8,128)(2,1)}, u32[]{:S(2)}) copy-start(bf16[2,16,1,256]{3,1,2,0:T(8,128)(2,1)} %maximum_bitcast_fusion.1) | copy-start | bytes 49156
  75.5 26.1 %copy-start.24 = (pred[16]{0:T(512)(128)(4,1)S(1)}, pred[16]{0:T(512)(128)(4,1)}, u32[]{:S(2)}) copy-start(pred[16]{0:T(512)(128)(4,1)} %get-tuple-element.15) | copy-start | bytes 52
  76.6 85.1 %all-gather.20.cloned.1.call-start = ((), (), s32[]{:S(2)}) async-start(), calls=%async_computation.4 | async-start | bytes 1179648 | tf_op jit(solution)/shard_map/all_gather | solution.py:15
  105.2 143.0 %all-gather.14.cloned.1.call-start = ((), (), s32[]{:S(2)}) async-start(), calls=%async_computation.1 | async-start | bytes 4325376 | tf_op jit(solution)/shard_map/all_gather | solution.py:118
  105.8 57.3 %copy-start.4 = (bf16[3,16,4096]{2,1,0:T(8,128)(2,1)S(1)}, bf16[3,16,4096]{2,1,0:T(8,128)(2,1)}, u32[]{:S(2)}) copy-start(bf16[3,16,4096]{2,1,0:T(8,128)(2,1)} %param.16) | copy-start | bytes 1179652
  105.8 188.5 %all-gather.12.cloned.1.call-start = ((), (), s32[]{:S(2)}) async-start(), calls=%async_computation | async-start | bytes 7077888 | tf_op jit(solution)/shard_map/all_gather | solution.py:120
  107.6 56.3 %copy-start.16 = (f32[4096]{0:T(1024)S(1)}, f32[4096]{0:T(1024)}, u32[]{:S(2)}) copy-start(f32[4096]{0:T(1024)} %param.24) | copy-start | bytes 49156
  196.4 27.0 %copy-start.25 = (f32[16]{0:T(128)S(1)}, f32[16]{0:T(128)}, u32[]{:S(2)}) copy-start(f32[16]{0:T(128)} %get-tuple-element.3) | copy-start | bytes 196
  248.1 53.7 %copy-start.20 = (pred[768]{0:T(1024)(128)(4,1)S(1)}, pred[768]{0:T(1024)(128)(4,1)}, u32[]{:S(2)}) copy-start(pred[768]{0:T(1024)(128)(4,1)} %iota_compare_fusion.2) | copy-start | bytes 2308
  (10 other events, 21.5 us)
Sparse Core Ops, SparseCore 0:
  46.7 38.6 all-gather.15
  87.2 35.8 all-gather.17
  124.8 36.8 all-gather.19
  164.1 55.0 all-gather.13
  220.8 73.4 all-gather.11
